TPU v7x, 32 devices: a whole 2x2x4 slice. The times are simulated.
32 devices in a mesh: bucket: 4 (over y, x), group: 8 (over z, core).
Axes of the slice: x: 2, y: 2, z: 4, core: 2. Of those that a mesh axis runs over, the one named last changes fastest.
Arguments:
- embeddings: bfloat16 [4, 8, 4, 128, 768], P('bucket', 'group'), may hold values from -6 to 6
- counts: int32 [4, 8, 4, 1], P('bucket', 'group'), may hold values from 42 to 128, as said below
Outputs:
- neighbour_sums: bfloat16 [4, 8, 512, 768], P('bucket', 'group')
Inputs may be any that keep to these rules, and one draw needn't show every extreme that they name: `counts`: each count is a live prefix of its 128 slots; in every draw some slot range is full.
All inputs are finite; a program needn't handle non-finite values.
Results may differ from a plain program's by a relative error of at most 0.0052.
Values may be sent and summed in bfloat16 or wider, within the bound.
No kernel may reach another device: no remote copies, remote signals or barrier semaphores. Data moves between devices by JAX's collectives and lax.ppermute only.
A program may use at most 128 MiB of HBM per device.

v0:
```python
import jax
import jax.numpy as jnp
from jax import lax
from jax.sharding import PartitionSpec as P

ROUNDS = 4
EPS = 1e-06
TEMP = 12.0


def normalize(block):
    values = block.astype(jnp.float32)
    return (values * lax.rsqrt(jnp.sum(values * values, axis=-1, keepdims=True) + EPS)).astype(
        jnp.bfloat16
    )


def weigh(unit_a, unit_b, live_b, extra):
    scores = jnp.dot(unit_a, unit_b.T, preferred_element_type=jnp.float32)
    return jnp.exp(TEMP * scores) * live_b[None, :] * extra


def per_device(embeddings, counts):
    slabs, slab_counts = (
        lax.all_to_all(embeddings, "bucket", split_axis=2, concat_axis=0, tiled=True),
        lax.all_to_all(counts, "bucket", split_axis=2, concat_axis=0, tiled=True),
    )
    sources = slabs.shape[0]
    slot_rows = slabs.shape[3]
    width = slabs.shape[4]
    rows = sources * slot_rows
    data = slabs.reshape(rows, width)
    slot_index = lax.broadcasted_iota(jnp.int32, (sources, slot_rows), 1)
    live = (slot_index < slab_counts.reshape(sources, 1)).astype(jnp.float32).reshape(rows)
    marks = live.astype(jnp.bfloat16)
    unit = normalize(data)
    not_self = 1.0 - jnp.eye(rows, dtype=jnp.float32)
    own = weigh(unit, unit, live, not_self)
    summed = jnp.dot(own.astype(jnp.bfloat16), data, preferred_element_type=jnp.float32)
    squares = jnp.sum(own * own, axis=1)
    all_data, all_marks = (
        lax.all_gather(data, "group", axis=0, tiled=True),
        lax.all_gather(marks, "group", axis=0, tiled=True),
    )
    blocks = lax.axis_size("group")
    position = lax.axis_index("group")
    for dist in range(1, ROUNDS + 1):
        for sign in (1, -1):
            other = (position + sign * dist) % blocks
            start = other * rows
            got_data = lax.dynamic_slice_in_dim(all_data, start, rows, 0)
            got_live = lax.dynamic_slice_in_dim(all_marks, start, rows, 0).astype(jnp.float32)
            weights = weigh(unit, normalize(got_data), got_live, 1.0)
            summed = summed + jnp.dot(
                weights.astype(jnp.bfloat16), got_data, preferred_element_type=jnp.float32
            )
            squares = squares + jnp.sum(weights * weights, axis=1)
    result = summed * lax.rsqrt(squares)[:, None] * live[:, None]
    return result.astype(jnp.bfloat16).reshape(1, 1, rows, width)


def solution(mesh):
    in_specs = (P("bucket", "group", None, None, None), P("bucket", "group", None, None))
    out_specs = P("bucket", "group", None, None)
    return jax.shard_map(
        per_device, mesh=mesh, in_specs=in_specs, out_specs=out_specs, check_vma=False
    )
```

profile of v0, /device:TPU:0, one launch (start us, length us, event | category | flops | bytes accessed | tf_op | source)
XLA Modules:
  0.0 112.1 jit_solution(2783596257850077988)
XLA Ops:
  6.5 0.0 copy-start.2
  6.5 0.0 all-gather.3.cloned.1.call-start
  6.5 17.3 %all_to_all.8 = bf16[1,1,4,128,768]{4,3,1,0,2:T(8,128)(2,1)} all-to-all(bf16[1,1,4,128,768]{4,3,1,0,2:T(8,128)(2,1)} %bitcast.36), channel_id=1, replica_groups=mesh['bucket'=4,'group'=8] {'bucket'}, dimensions={2} | all-to-all | bytes 1572864 | tf_op jit(solution)/shard_map/all_to_all | solution.py:25
  23.8 0.0 copy-start
  23.8 0.0 all-gather.3.cloned.1.call-update
  23.9 0.0 copy-done.2
  23.9 0.7 copy.6
  24.5 3.2 %all-to-all-start.1 = ((s32[1,1,4,1]{3,1,0,2:T(1,128)}), s32[1,1,4,1]{3,1,0,2:T(1,128)S(1)}, u32[]{:S(2)}, u32[]{:S(2)}) async-start(s32[1,1,4,1]{3,1,0,2:T(1,128)} %copy.6), calls=%async_computation.1 | async-start | bytes 4096 | tf_op jit(solution)/shard_map/all_to_all | solution.py:26
  27.9 4.4 %all-to-all-done.1 = s32[1,1,4,1]{3,1,0,2:T(1,128)S(1)} async-done(((s32[1,1,4,1]{3,1,0,2:T(1,128)}), s32[1,1,4,1]{3,1,0,2:T(1,128)S(1)}, u32[]{:S(2)}, u32[]{:S(2)}) %all-to-all-start.1) | async-done | bytes 48 | tf_op jit(solution)/shard_map/all_to_all | solution.py:26
  32.3 0.2 reduce.1
  32.5 0.1 convert_bitcast_fusion
  32.6 13.6 %all-gather = bf16[8,1,512]{2,1,0:T(2,128)(2,1)S(1)} all-gather(bf16[1,1,512]{2,1,0:T(2,128)(2,1)S(1)} %reshape.165), channel_id=1, replica_groups=mesh['bucket'=4,'group'=8] {'group'}, dimensions={0}, use_global_device_ids=true | all-gather | bytes 9216 | tf_op jit(solution)/shard_map/all_gather | solution.py:43
  46.3 0.1 dynamic-slice_convert_fusion
  46.4 0.0 copy-done
  46.4 0.2 fusion
  46.6 0.2 multiply_convert_fusion.1
  46.8 0.2 fusion.1
  47.0 0.7 multiply_reduce_fusion.8
  47.8 0.6 fusion.85
  48.4 40.3 %all-gather.3.cloned.1.call-done = bf16[4096,768]{1,0:T(8,128)(2,1)} async-done(((bf16[512,768]{1,0:T(8,128)(2,1)}), bf16[4096,768]{1,0:T(8,128)(2,1)}) %all-gather.3.cloned.1.call-update) | async-done | bytes 6291472 | tf_op jit(solution)/shard_map/all_gather | solution.py:42
  88.6 0.0 copy-start.1
  88.6 4.2 %fusion.16 = (f32[512]{0:T(512)S(1)}, f32[512]{0:T(512)S(1)}, f32[512]{0:T(512)S(1)}, f32[512]{0:T(512)S(1)}, f32[512]{0:T(512)S(1)}, /*index=5*/f32[512]{0:T(512)S(1)}, f32[512]{0:T(512)S(1)}, f32[512]{0:T(512)S(1)}) fusion(bf16[4096,768]{1,0:T(8,128)(2,1)} %all-gather.3.cloned.1.call-done, s32[]{:T(128)S(6)} %select_n.82, s32[]{:T(128)S(6)} %select_n.80, ...), kind=kLoop, calls=%fused_computation.34 | loop fusion | flops 9433088 | bytes 6307872 | tf_op jit(solution)/shard_map/reduce_sum | solution.py:13
  93.0 0.4 copy-done.1
  93.3 0.7 multiply_reduce_fusion.1
  94.0 0.7 multiply_reduce_fusion.2
  94.8 0.7 multiply_reduce_fusion.3
  95.5 0.7 multiply_reduce_fusion.4
  96.2 0.7 multiply_reduce_fusion.5
  97.0 0.7 multiply_reduce_fusion.6
  97.7 0.7 multiply_reduce_fusion.7
  98.4 0.7 multiply_reduce_fusion
  99.2 0.6 fusion.57
  99.8 0.6 fusion.60
  100.4 0.6 fusion.63
  101.0 0.6 fusion.66
  101.6 0.6 fusion.69
  102.2 0.6 fusion.72
  102.8 0.6 fusion.75
  103.4 1.8 %fusion.37 = bf16[1,1,512,768]{3,2,1,0:T(8,128)(2,1)} fusion(f32[512,768]{1,0:T(8,128)S(1)} %fusion.57, f32[512,768]{1,0:T(8,128)S(1)} %fusion.60, f32[512,768]{1,0:T(8,128)S(1)} %fusion.63, f32[512,768]{1,0:T(8,128)S(1)} %fusion.66, f32[512,768]{1,0:T(8,128)S(1)} %fusion.69, f32[512,768]{1,0:T(8,128)S(1)} %fusion.72, f32[512,768]{1,0:T(8,128)S(1)} %fusion.85, ...), kind=kOutput, calls=%fused_computation.66 | convolution fusion | flops 406978560 | bytes 14684164 | tf_op jit(solution)/shard_map/dot_general | solution.py:54
  (9 shorter events, 0.1 us)
Async XLA Ops:
  6.5 17.3 %copy-start.2 = (s32[1,1,4,1]{2,3,1,0:T(1,128)S(1)}, s32[1,1,4,1]{2,3,1,0:T(1,128)}, u32[]{:S(2)}) copy-start(s32[1,1,4,1]{2,3,1,0:T(1,128)} %param.3) | copy-start | bytes 52
  6.5 82.1 %all-gather.3.cloned.1.call-start = ((), (), s32[]{:S(2)}) async-start(), calls=%async_computation.2 | async-start | bytes 7077888 | tf_op jit(solution)/shard_map/all_gather | solution.py:42
  23.8 22.5 %copy-start = (bf16[1,1,4,128,768]{4,3,1,0,2:T(8,128)(2,1)S(1)}, bf16[1,1,4,128,768]{4,3,1,0,2:T(8,128)(2,1)}, u32[]{:S(2)}) copy-start(bf16[1,1,4,128,768]{4,3,1,0,2:T(8,128)(2,1)} %all_to_all.8) | copy-start | bytes 2359300
  24.5 7.8 %all-to-all-start.1 = ((s32[1,1,4,1]{3,1,0,2:T(1,128)}), s32[1,1,4,1]{3,1,0,2:T(1,128)S(1)}, u32[]{:S(2)}, u32[]{:S(2)}) async-start(s32[1,1,4,1]{3,1,0,2:T(1,128)} %copy.6), calls=%async_computation.1 | async-start | bytes 4096 | tf_op jit(solution)/shard_map/all_to_all | solution.py:26
  88.6 4.7 %copy-start.1 = (bf16[4096,768]{1,0:T(8,128)(2,1)S(1)}, bf16[4096,768]{1,0:T(8,128)(2,1)}, u32[]{:S(2)}) copy-start(bf16[4096,768]{1,0:T(8,128)(2,1)} %all-gather.3.cloned.1.call-done) | copy-start | bytes 18874372
Sparse Core Ops, SparseCore 0:
  24.0 64.6 all-gather.2
where the time goes:
time: 112 us
  waiting for transfers between devices  44.7 us (40%)
  blocking collectives  30.9 us (28%)
  between operations  13.7 us (12%)
  matrix products  13.2 us (12%)
  other arithmetic  5.33 us (5%)
  starting transfers between devices  3.22 us (3%)
    all_gather x1, waiting for transfers between devices, per_device(): lax.all_gather(data, 'group', axis=0, tiled=True)  40.3 us
    all_to_all x1, blocking collectives, per_device(): lax.all_to_all(embeddings, 'bucket', split_axis=2, concat_axis=0, tiled=T...  17.3 us
    all_gather x1, blocking collectives, per_device(): lax.all_gather(marks, 'group', axis=0, tiled=True)  13.6 us
    dot_general x9, matrix products, weigh(): scores = jnp.dot(unit_a, unit_b.T, preferred_element_type=jnp.float32)  6.57 us
    dot_general x8, matrix products, per_device(): jnp.dot(weights.astype(jnp.bfloat16), got_data, preferred_element_type=jn...  6.04 us
    reduce_sum x2, other arithmetic, normalize(): jnp.sum(values * values, axis=-1, keepdims=True) + EPS  4.47 us
    all_to_all x1, waiting for transfers between devices, per_device(): lax.all_to_all(counts, 'bucket', split_axis=2, concat_axis=0, tiled=True)  4.43 us
    all_to_all x1, starting transfers between devices, per_device(): lax.all_to_all(counts, 'bucket', split_axis=2, concat_axis=0, tiled=True)  3.22 us
  transfers between devices with their start and end apart: 2, of which 2 were waited for; matrix products, arithmetic and copies ran while one was open for 3% of the time, Pallas kernels for 0%

commit v1 on v0

--- a/solution.py
+++ b/solution.py
@@ -6,6 +6,27 @@
 ROUNDS = 4
 EPS = 1e-06
 TEMP = 12.0
+
+
+def gather_around(x, axis, dim):
+    size, position, extent = (lax.axis_size(axis), lax.axis_index(axis), x.shape[dim])
+    right = [(i, (i + 1) % size) for i in range(size)]
+    backward = [(i, (i - 1) % size) for i in range(size)]
+    whole = jnp.zeros((*x.shape[:dim], size * extent, *x.shape[dim + 1 :]), x.dtype)
+    whole = lax.dynamic_update_slice_in_dim(whole, x, position * extent, axis=dim)
+    from_left = from_right = x
+    halfway = size // 2
+    for step in range(1, halfway + 1):
+        from_left = lax.ppermute(from_left, axis, right)
+        whole = lax.dynamic_update_slice_in_dim(
+            whole, from_left, (position - step) % size * extent, axis=dim
+        )
+        if step < size - halfway:
+            from_right = lax.ppermute(from_right, axis, backward)
+            whole = lax.dynamic_update_slice_in_dim(
+                whole, from_right, (position + step) % size * extent, axis=dim
+            )
+    return whole
 
 
 def normalize(block):
@@ -39,7 +60,7 @@
     summed = jnp.dot(own.astype(jnp.bfloat16), data, preferred_element_type=jnp.float32)
     squares = jnp.sum(own * own, axis=1)
     all_data, all_marks = (
-        lax.all_gather(data, "group", axis=0, tiled=True),
+        gather_around(data, "group", 0),
         lax.all_gather(marks, "group", axis=0, tiled=True),
     )
     blocks = lax.axis_size("group")

time: 112 us -> 107 us (0.955)
  between operations: 13.7 us -> 0.36 us
  blocking collectives: 30.9 us -> 40 us
  starting transfers between devices: 3.22 us -> 11.3 us
  waiting for transfers between devices: 44.7 us -> 37.6 us
  other arithmetic: 5.33 us -> 2.41 us
    all_gather x1 -> x0, waiting for transfers between devices: 40.3 us -> none  [per_device(): lax.all_gather(data, 'group', axis=0, tiled=True)]
    ppermute x0 -> x7, waiting for transfers between devices: none -> 33.1 us  [the longest x3 30.9 us: gather_around(): from_right = lax.ppermute(from_right, axis, backward)]
    all_gather x1, blocking collectives: 13.6 us -> 23.4 us  [per_device(): lax.all_gather(marks, 'group', axis=0, tiled=True)]
    ppermute x0 -> x7, starting transfers between devices: none -> 8.11 us  [the longest x3 7.86 us: gather_around(): from_right = lax.ppermute(from_right, axis, backward)]
    reduce_sum x2, other arithmetic: 4.47 us -> 1.56 us  [normalize(): jnp.sum(values * values, axis=-1, keepdims=True) + EPS]
  transfers between devices with their start and end apart: 2 -> 8, of which waited for: 2 -> 4; matrix products, arithmetic and copies ran while one was open for 3% -> 4% of each run, Pallas kernels for 0% -> 0%
where the time goes in v1:
time: 107 us
  blocking collectives  40 us (37%)
  waiting for transfers between devices  37.6 us (35%)
  matrix products  13.4 us (13%)
  starting transfers between devices  11.3 us (11%)
  other arithmetic  2.41 us (2%)
  local copies, waits for them, and re-layouts  1.59 us (1%)
    ppermute x3, waiting for transfers between devices, gather_around(): from_right = lax.ppermute(from_right, axis, backward)  30.9 us
    all_gather x1, blocking collectives, per_device(): lax.all_gather(marks, 'group', axis=0, tiled=True)  23.4 us
    all_to_all x1, blocking collectives, per_device(): lax.all_to_all(embeddings, 'bucket', split_axis=2, concat_axis=0, tiled=T...  16.7 us
    ppermute x3, starting transfers between devices, gather_around(): from_right = lax.ppermute(from_right, axis, backward)  7.86 us
    dot_general x9, matrix products, weigh(): scores = jnp.dot(unit_a, unit_b.T, preferred_element_type=jnp.float32)  6.57 us
    dot_general x8, matrix products, per_device(): jnp.dot(weights.astype(jnp.bfloat16), got_data, preferred_element_type=jn...  6.27 us
    all_to_all x1, waiting for transfers between devices, per_device(): lax.all_to_all(counts, 'bucket', split_axis=2, concat_axis=0, tiled=True)  4.42 us
    all_to_all x1, starting transfers between devices, per_device(): lax.all_to_all(counts, 'bucket', split_axis=2, concat_axis=0, tiled=True)  3.22 us
  transfers between devices with their start and end apart: 8, of which 4 were waited for; matrix products, arithmetic and copies ran while one was open for 4% of the time, Pallas kernels for 0%

profile of v1, /device:TPU:0, one launch (start us, length us, event | category | flops | bytes accessed | tf_op | source)
XLA Modules:
  0.0 106.7 jit_solution(9111560680733446689)
XLA Ops:
  0.0 0.0 copy-start
  0.0 16.7 %all_to_all.8 = bf16[1,1,4,128,768]{4,3,1,0,2:T(8,128)(2,1)S(1)} all-to-all(bf16[1,1,4,128,768]{4,3,1,0,2:T(8,128)(2,1)} %bitcast.38), channel_id=1, replica_groups=mesh['bucket'=4,'group'=8] {'bucket'}, dimensions={2} | all-to-all | bytes 1572864 | tf_op jit(solution)/shard_map/all_to_all | solution.py:46
  16.7 0.0 collective-permute-start
  16.7 0.0 copy-done
  16.7 0.7 copy.6
  17.3 3.2 %all-to-all-start.1 = ((s32[1,1,4,1]{3,1,0,2:T(1,128)}), s32[1,1,4,1]{3,1,0,2:T(1,128)S(1)}, u32[]{:S(2)}, u32[]{:S(2)}) async-start(s32[1,1,4,1]{3,1,0,2:T(1,128)} %copy.6), calls=%async_computation.1 | async-start | bytes 4096 | tf_op jit(solution)/shard_map/all_to_all | solution.py:47
  20.7 4.4 %all-to-all-done.1 = s32[1,1,4,1]{3,1,0,2:T(1,128)S(1)} async-done(((s32[1,1,4,1]{3,1,0,2:T(1,128)}), s32[1,1,4,1]{3,1,0,2:T(1,128)S(1)}, u32[]{:S(2)}, u32[]{:S(2)}) %all-to-all-start.1) | async-done | bytes 48 | tf_op jit(solution)/shard_map/all_to_all | solution.py:47
  25.1 0.2 reduce.1
  25.3 2.4 %collective-permute-start.1 = (bf16[512,768]{1,0:T(8,128)(2,1)S(1)}, bf16[512,768]{1,0:T(8,128)(2,1)S(1)}, u32[]{:S(2)}, u32[]{:S(2)}) collective-permute-start(bf16[512,768]{1,0:T(8,128)(2,1)S(1)} %bitcast.35), channel_id=1, source_target_pairs={{0,7},{1,0},{2,1},{3,2},{4,3},{5,4},{6,5},{7,6},{8,15},{9,8},{10,9... | collective-permute-start | bytes 2359304 | tf_op jit(solution)/shard_map/ppermute | solution.py:25
  27.7 2.2 %collective-permute-done = bf16[512,768]{1,0:T(8,128)(2,1)S(1)} collective-permute-done((bf16[512,768]{1,0:T(8,128)(2,1)S(1)}, bf16[512,768]{1,0:T(8,128)(2,1)S(1)}, u32[]{:S(2)}, u32[]{:S(2)}) %collective-permute-start) | collective-permute-done | bytes 786464 | tf_op jit(solution)/shard_map/ppermute | solution.py:20
  29.9 0.0 collective-permute-start.2
  29.9 0.1 fusion.106
  30.0 23.4 %all-gather = bf16[8,1,512]{2,1,0:T(2,128)(2,1)S(1)} all-gather(bf16[1,1,512]{2,1,0:T(2,128)(2,1)S(1)} %reshape.165), channel_id=1, replica_groups=mesh['bucket'=4,'group'=8] {'group'}, dimensions={0}, use_global_device_ids=true | all-gather | bytes 9216 | tf_op jit(solution)/shard_map/all_gather | solution.py:64
  53.5 0.1 dynamic-slice_convert_fusion.7
  53.6 0.2 fusion
  53.8 0.2 multiply_convert_fusion.1
  54.0 0.0 collective-permute-done.1
  54.0 1.7 %collective-permute-start.3 = (bf16[512,768]{1,0:T(8,128)(2,1)S(1)}, bf16[512,768]{1,0:T(8,128)(2,1)S(1)}, u32[]{:S(2)}, u32[]{:S(2)}) collective-permute-start(bf16[512,768]{1,0:T(8,128)(2,1)S(1)} %collective-permute-done.1), channel_id=1, source_target_pairs={{0,7},{1,0},{2,1},{3,2},{4,3},{5,4},{6,5},{7,6},{8,15},{9,8},{10,9... | collective-permute-start | bytes 2359304 | tf_op jit(solution)/shard_map/ppermute | solution.py:25
  55.8 0.0 collective-permute-done.2
  55.8 0.0 collective-permute-start.4
  55.8 0.2 fusion.1
  56.0 0.8 multiply_reduce_fusion.8
  56.7 0.6 fusion.88
  57.3 16.1 %collective-permute-done.3 = bf16[512,768]{1,0:T(8,128)(2,1)S(1)} collective-permute-done((bf16[512,768]{1,0:T(8,128)(2,1)S(1)}, bf16[512,768]{1,0:T(8,128)(2,1)S(1)}, u32[]{:S(2)}, u32[]{:S(2)}) %collective-permute-start.3) | collective-permute-done | bytes 786464 | tf_op jit(solution)/shard_map/ppermute | solution.py:25
  73.4 3.7 %collective-permute-start.5 = (bf16[512,768]{1,0:T(8,128)(2,1)S(1)}, bf16[512,768]{1,0:T(8,128)(2,1)S(1)}, u32[]{:S(2)}, u32[]{:S(2)}) collective-permute-start(bf16[512,768]{1,0:T(8,128)(2,1)S(1)} %collective-permute-done.3), channel_id=1, source_target_pairs={{0,7},{1,0},{2,1},{3,2},{4,3},{5,4},{6,5},{7,6},{8,15},{9,8},{10,9... | collective-permute-start | bytes 2359304 | tf_op jit(solution)/shard_map/ppermute | solution.py:25
  77.1 0.4 broadcast_in_dim.2
  77.6 0.1 constant_dynamic-update-slice_fusion.7
  77.6 0.0 collective-permute-done.4
  77.6 0.2 collective-permute-start.6
  77.9 0.1 constant_dynamic-update-slice_fusion.6
  78.0 0.1 constant_dynamic-update-slice_fusion.5
  78.0 0.1 constant_dynamic-update-slice_fusion.4
  78.1 0.1 constant_dynamic-update-slice_fusion.3
  78.2 0.1 constant_dynamic-update-slice_fusion.2
  78.2 14.8 %collective-permute-done.5 = bf16[512,768]{1,0:T(8,128)(2,1)S(1)} collective-permute-done((bf16[512,768]{1,0:T(8,128)(2,1)S(1)}, bf16[512,768]{1,0:T(8,128)(2,1)S(1)}, u32[]{:S(2)}, u32[]{:S(2)}) %collective-permute-start.5) | collective-permute-done | bytes 786464 | tf_op jit(solution)/shard_map/ppermute | solution.py:25
  93.1 0.1 constant_dynamic-update-slice_fusion.1
  93.1 0.0 collective-permute-done.6
  93.1 0.1 constant_dynamic-update-slice_fusion
  93.2 1.3 %fusion.2 = (f32[512]{0:T(512)S(1)}, f32[512]{0:T(512)S(1)}, f32[512]{0:T(512)S(1)}, f32[512]{0:T(512)S(1)}, f32[512]{0:T(512)S(1)}, /*index=5*/f32[512]{0:T(512)S(1)}, f32[512]{0:T(512)S(1)}, f32[512]{0:T(512)S(1)}) fusion(bf16[4096,768]{1,0:T(8,128)(2,1)S(1)} %constant_dynamic-update-slice_fusion, s32[]{:T(128)S(6)} %select_n.95, s32[]{:T(128)S(6)} %select_n.105, ...), kind=kLoop, calls=%fused_computation.20 | loop fusion | flops 9433088 | bytes 6307872 | tf_op jit(solution)/shard_map/reduce_sum | solution.py:34
  94.6 0.7 multiply_reduce_fusion.1
  95.3 0.6 fusion.60
  95.9 0.7 multiply_reduce_fusion.2
  96.6 0.6 fusion.63
  97.3 0.7 multiply_reduce_fusion.3
  98.0 0.6 fusion.66
  98.6 0.7 multiply_reduce_fusion.4
  99.3 0.6 fusion.69
  99.9 0.7 multiply_reduce_fusion.5
  100.7 0.6 fusion.72
  101.3 0.7 multiply_reduce_fusion.6
  102.0 0.6 fusion.75
  102.6 0.7 multiply_reduce_fusion.7
  103.3 0.6 fusion.78
  103.9 0.7 multiply_reduce_fusion
  104.7 2.1 %fusion.53 = bf16[1,1,512,768]{3,2,1,0:T(8,128)(2,1)} fusion(f32[512]{0:T(512)S(1)} %get-tuple-element.24, f32[512]{0:T(512)S(1)} %add_rsqrt_fusion, f32[512,768]{1,0:T(8,128)S(1)} %fusion.60, f32[512,768]{1,0:T(8,128)S(1)} %fusion.63, f32[512,768]{1,0:T(8,128)S(1)} %fusion.66, f32[512,768]{1,0:T(8,128)S(1)} %fusion.69, f32[512,768]{1,0:T(8,128)S(1)} %fusion.72, ...), kind=kOutput, calls=%fused_computation.84 | convolution fusion | flops 406978560 | bytes 14684164 | tf_op jit(solution)/shard_map/dot_general | solution.py:75
  (9 shorter events, 0.1 us)
Async XLA Ops:
  0.0 16.7 %copy-start = (s32[1,1,4,1]{2,3,1,0:T(1,128)S(1)}, s32[1,1,4,1]{2,3,1,0:T(1,128)}, u32[]{:S(2)}) copy-start(s32[1,1,4,1]{2,3,1,0:T(1,128)} %param.3) | copy-start | bytes 52
  16.7 13.3 %collective-permute-start = (bf16[512,768]{1,0:T(8,128)(2,1)S(1)}, bf16[512,768]{1,0:T(8,128)(2,1)S(1)}, u32[]{:S(2)}, u32[]{:S(2)}) collective-permute-start(bf16[512,768]{1,0:T(8,128)(2,1)S(1)} %bitcast.34), channel_id=1, source_target_pairs={{0,1},{1,2},{2,3},{3,4},{4,5},{5,6},{6,7},{7,0},{8,9},{9,10},{10,1... | collective-permute-start | bytes 2359304 | tf_op jit(solution)/shard_map/ppermute | solution.py:20
  17.3 7.8 %all-to-all-start.1 = ((s32[1,1,4,1]{3,1,0,2:T(1,128)}), s32[1,1,4,1]{3,1,0,2:T(1,128)S(1)}, u32[]{:S(2)}, u32[]{:S(2)}) async-start(s32[1,1,4,1]{3,1,0,2:T(1,128)} %copy.6), calls=%async_computation.1 | async-start | bytes 4096 | tf_op jit(solution)/shard_map/all_to_all | solution.py:47
  25.3 28.8 %collective-permute-start.1 = (bf16[512,768]{1,0:T(8,128)(2,1)S(1)}, bf16[512,768]{1,0:T(8,128)(2,1)S(1)}, u32[]{:S(2)}, u32[]{:S(2)}) collective-permute-start(bf16[512,768]{1,0:T(8,128)(2,1)S(1)} %bitcast.35), channel_id=1, source_target_pairs={{0,7},{1,0},{2,1},{3,2},{4,3},{5,4},{6,5},{7,6},{8,15},{9,8},{10,9... | collective-permute-start | bytes 2359304 | tf_op jit(solution)/shard_map/ppermute | solution.py:25
  29.9 25.8 %collective-permute-start.2 = (bf16[512,768]{1,0:T(8,128)(2,1)S(1)}, bf16[512,768]{1,0:T(8,128)(2,1)S(1)}, u32[]{:S(2)}, u32[]{:S(2)}) collective-permute-start(bf16[512,768]{1,0:T(8,128)(2,1)S(1)} %collective-permute-done), channel_id=1, source_target_pairs={{0,1},{1,2},{2,3},{3,4},{4,5},{5,6},{6,7},{7,0},{8,9},{9,10},{10,1... | collective-permute-start | bytes 2359304 | tf_op jit(solution)/shard_map/ppermute | solution.py:20
  54.0 19.4 %collective-permute-start.3 = (bf16[512,768]{1,0:T(8,128)(2,1)S(1)}, bf16[512,768]{1,0:T(8,128)(2,1)S(1)}, u32[]{:S(2)}, u32[]{:S(2)}) collective-permute-start(bf16[512,768]{1,0:T(8,128)(2,1)S(1)} %collective-permute-done.1), channel_id=1, source_target_pairs={{0,7},{1,0},{2,1},{3,2},{4,3},{5,4},{6,5},{7,6},{8,15},{9,8},{10,9... | collective-permute-start | bytes 2359304 | tf_op jit(solution)/shard_map/ppermute | solution.py:25
  55.8 21.9 %collective-permute-start.4 = (bf16[512,768]{1,0:T(8,128)(2,1)S(1)}, bf16[512,768]{1,0:T(8,128)(2,1)S(1)}, u32[]{:S(2)}, u32[]{:S(2)}) collective-permute-start(bf16[512,768]{1,0:T(8,128)(2,1)S(1)} %collective-permute-done.2), channel_id=1, source_target_pairs={{0,1},{1,2},{2,3},{3,4},{4,5},{5,6},{6,7},{7,0},{8,9},{9,10},{10,1... | collective-permute-start | bytes 2359304 | tf_op jit(solution)/shard_map/ppermute | solution.py:20
  73.4 19.6 %collective-permute-start.5 = (bf16[512,768]{1,0:T(8,128)(2,1)S(1)}, bf16[512,768]{1,0:T(8,128)(2,1)S(1)}, u32[]{:S(2)}, u32[]{:S(2)}) collective-permute-start(bf16[512,768]{1,0:T(8,128)(2,1)S(1)} %collective-permute-done.3), channel_id=1, source_target_pairs={{0,7},{1,0},{2,1},{3,2},{4,3},{5,4},{6,5},{7,6},{8,15},{9,8},{10,9... | collective-permute-start | bytes 2359304 | tf_op jit(solution)/shard_map/ppermute | solution.py:25
  77.6 15.5 %collective-permute-start.6 = (bf16[512,768]{1,0:T(8,128)(2,1)S(1)}, bf16[512,768]{1,0:T(8,128)(2,1)S(1)}, u32[]{:S(2)}, u32[]{:S(2)}) collective-permute-start(bf16[512,768]{1,0:T(8,128)(2,1)S(1)} %collective-permute-done.4), channel_id=1, source_target_pairs={{0,1},{1,2},{2,3},{3,4},{4,5},{5,6},{6,7},{7,0},{8,9},{9,10},{10,1... | collective-permute-start | bytes 2359304 | tf_op jit(solution)/shard_map/ppermute | solution.py:20
